TPU v7x, 256 devices: a whole 4x4x8 slice. The times are simulated.
256 devices in a mesh: tm: 16 (over z, core), head: 16 (over y, x).
Axes of the slice: x: 4, y: 4, z: 8, core: 2. Of those that a mesh axis runs over, the one named last changes fastest.
Arguments:
- frames: bfloat16 [8192, 2048], P(('tm', 'head')), may hold values from -6 to 6
- log_decay: float32 [8192, 16], P('tm', 'head'), may hold values from -2 to 0, as said below
- w_query: bfloat16 [2048, 2048], P('tm', 'head'), may hold values from -0.125 to 0.125
- w_key: bfloat16 [2048, 2048], P('tm', 'head'), may hold values from -0.125 to 0.125
- w_value: bfloat16 [2048, 2048], P('tm', 'head'), may hold values from -0.125 to 0.125
- w_gate: bfloat16 [2048, 2048], P('tm', 'head'), may hold values from -0.125 to 0.125
- w_out: bfloat16 [2048, 2048], P('head', 'tm'), may hold values from -0.125 to 0.125
Outputs:
- mixed: bfloat16 [8192, 2048], P(('tm', 'head'))
Inputs may be any that keep to these rules, and one draw needn't show every extreme that they name: `log_decay`: strictly negative.
All inputs are finite; a program needn't handle non-finite values.
Results may differ from a plain program's by a relative error of at most 0.015.
Values may be sent and summed in bfloat16 or wider, within the bound.
No kernel may reach another device: no remote copies, remote signals or barrier semaphores. Data moves between devices by JAX's collectives and lax.ppermute only.
A program may use at most 64 MiB of HBM per device.

v0:
```python
import jax
import jax.numpy as jnp
from jax import lax
from jax.sharding import PartitionSpec as P

HEAD_DIM = 128
BLOCK = 512
PAD_ROWS = 8


def gather_by_exchange(part, axis):
    count = lax.axis_size(axis)
    copies = jnp.broadcast_to(part[None], (count,) + part.shape)
    return lax.all_to_all(copies, axis, 0, 0, tiled=False)


def prior_state(local_final, log_total, axis):
    heads_here = local_final.shape[0]
    high = log_total.astype(jnp.bfloat16)
    low = (log_total - high.astype(jnp.float32)).astype(jnp.bfloat16)
    extra = jnp.concatenate(
        [
            jnp.broadcast_to(high[:, None, None], (heads_here, 1, HEAD_DIM)),
            jnp.broadcast_to(low[:, None, None], (heads_here, 1, HEAD_DIM)),
            jnp.zeros((heads_here, PAD_ROWS - 2, HEAD_DIM), jnp.bfloat16),
        ],
        axis=1,
    )
    packed = jnp.concatenate([local_final.astype(jnp.bfloat16), extra], axis=1)
    gathered = gather_by_exchange(packed, axis)
    finals = gathered[:, :, :HEAD_DIM, :].astype(jnp.float32)
    totals = gathered[:, :, HEAD_DIM, 0].astype(jnp.float32) + gathered[
        :, :, HEAD_DIM + 1, 0
    ].astype(jnp.float32)
    count = gathered.shape[0]
    mine = lax.axis_index(axis)
    order = jnp.arange(count, dtype=jnp.int32)
    between = (order[:, None] < order[None, :]) & (order[None, :] < mine)
    exponent = jnp.sum(jnp.where(between[:, :, None], totals[None, :, :], 0.0), axis=1)
    weight = jnp.where((order < mine)[:, None], jnp.exp(exponent), 0.0)
    return jnp.sum(weight[:, :, None, None] * finals, axis=0)


def shards(frames, log_decay, w_query, w_key, w_value, w_gate, w_out):
    head_width = w_query.shape[1]
    blocks = [w_query, w_key, w_value, w_gate, w_out]
    width = sum((block.shape[1] for block in blocks))
    column = jnp.arange(width)[None, :]
    packed = jnp.pad(blocks[-1], ((0, 0), (width - head_width, 0)))
    for start, block in reversed(list(zip(range(0, width, head_width), blocks))[:-1]):
        padded = jnp.pad(block, ((0, 0), (start, width - start - head_width)))
        packed = jnp.where(column < start + head_width, padded, packed)
    stacked = lax.all_gather(packed, "tm", axis=0, tiled=True)
    joined = stacked[:, : 4 * head_width]
    out_blocks = stacked[:, 4 * head_width :].reshape(-1, head_width, w_out.shape[1])
    frames_here = gather_by_exchange(frames, "head").reshape(-1, frames.shape[1])
    projected = jnp.dot(frames_here, joined, preferred_element_type=jnp.float32)
    local_len = projected.shape[0]
    heads_here = head_width // HEAD_DIM
    block_count = local_len // BLOCK
    query_blocks = (
        projected[:, :head_width]
        .astype(jnp.bfloat16)
        .reshape(block_count, BLOCK, heads_here, HEAD_DIM)
    )
    key_blocks = (
        projected[:, head_width : 2 * head_width]
        .astype(jnp.bfloat16)
        .reshape(block_count, BLOCK, heads_here, HEAD_DIM)
    )
    value_blocks = (
        projected[:, 2 * head_width : 3 * head_width]
        .astype(jnp.bfloat16)
        .reshape(block_count, BLOCK, heads_here, HEAD_DIM)
    )
    gate_all = projected[:, 3 * head_width :]
    running_blocks = jnp.cumsum(log_decay.reshape(block_count, BLOCK, heads_here), axis=1)
    slice_ordinal = jnp.arange(BLOCK, dtype=jnp.int32)
    causal = slice_ordinal[:, None] >= slice_ordinal[None, :]

    def local_step(carry_state, inputs):
        query_block, key_block, value_block, running = inputs
        gaps = running.T[:, :, None] - running.T[:, None, :]
        decay = jnp.exp(jnp.where(causal[None], gaps, -jnp.inf))
        scores = jnp.einsum(
            "thd,shd->hts", query_block, key_block, preferred_element_type=jnp.float32
        )
        weights = (scores * decay).astype(jnp.bfloat16)
        intra = jnp.einsum("hts,shd->thd", weights, value_block, preferred_element_type=jnp.float32)
        scaled = (
            key_block.astype(jnp.float32) * jnp.exp(running[-1][None, :] - running)[:, :, None]
        ).astype(jnp.bfloat16)
        update = jnp.einsum("shd,she->hde", scaled, value_block, preferred_element_type=jnp.float32)
        next_state = jnp.exp(running[-1])[:, None, None] * carry_state + update
        return (next_state, (intra, carry_state))

    zero_state = jnp.zeros((heads_here, HEAD_DIM, HEAD_DIM), jnp.float32)
    local_final, (intra_all, local_starts) = lax.scan(
        local_step, zero_state, (query_blocks, key_blocks, value_blocks, running_blocks)
    )
    prior = prior_state(local_final, jnp.sum(log_decay, axis=0), "tm")
    block_logs = running_blocks[:, -1, :]
    before = jnp.cumsum(block_logs, axis=0) - block_logs
    start_states = jnp.exp(before)[:, :, None, None] * prior[None] + local_starts
    lifted = query_blocks.astype(jnp.float32) * jnp.exp(running_blocks)[..., None]
    inter = jnp.einsum("cthd,chde->cthe", lifted, start_states, precision=lax.Precision.HIGHEST)
    retained = (intra_all + inter).reshape(local_len, heads_here, HEAD_DIM)
    center = jnp.mean(retained, axis=-1, keepdims=True)
    spread = jnp.mean((retained - center) ** 2, axis=-1, keepdims=True)
    normed = (retained - center) / jnp.sqrt(spread + 1e-05)
    gated = (
        (jax.nn.silu(gate_all.reshape(local_len, heads_here, HEAD_DIM)) * normed)
        .astype(jnp.bfloat16)
        .reshape(local_len, head_width)
    )
    heads = lax.axis_size("head")
    side = int(round(heads**0.5))
    me = lax.axis_index("head")
    row, col = (me // side, me % side)
    rows_mine = out_blocks
    ring_order = sorted(range(1, side), key=lambda shift: -min(shift, side - shift))
    by_owner = gated.reshape(side, side, local_len // heads, head_width)
    units = lax.axis_size("tm")
    half = rows_mine.shape[0] // 2
    parity = lax.axis_index("tm") % 2
    own_half = lax.dynamic_slice_in_dim(rows_mine, parity * half, half, axis=0)
    pieces = [lax.dynamic_index_in_dim(by_owner, col, axis=1, keepdims=False)]
    fetched = []
    for shift in ring_order:
        across = [(h, h // side * side + (h % side + shift) % side) for h in range(heads)]
        piece = lax.dynamic_index_in_dim(by_owner, (col + shift) % side, axis=1, keepdims=False)
        pieces.append(lax.ppermute(piece, "head", across))
        fetched.append(lax.ppermute(own_half, "head", across))
    fetched = jnp.stack(fetched)
    swapped = lax.ppermute(fetched, "tm", [(t, t ^ 1) for t in range(units)])
    first = jnp.where(parity == 0, fetched, swapped)
    second = jnp.where(parity == 0, swapped, fetched)
    remote = jnp.concatenate([first, second], axis=1)
    weights_in = [rows_mine] + [remote[s] for s in range(side - 1)]
    partial = jnp.einsum(
        "syfr,skrc->yfkc",
        jnp.stack(pieces),
        jnp.stack(weights_in),
        preferred_element_type=jnp.float32,
    ).astype(jnp.bfloat16)
    partial = partial.reshape(side, local_len // heads, -1)
    total = lax.dynamic_index_in_dim(partial, row, axis=0, keepdims=False).astype(jnp.float32)
    for shift in ring_order:
        down = [(h, (h // side + shift) % side * side + h % side) for h in range(heads)]
        piece = lax.dynamic_index_in_dim(partial, (row + shift) % side, axis=0, keepdims=False)
        total = total + lax.ppermute(piece, "head", down).astype(jnp.float32)
    return total.astype(jnp.bfloat16)


def solution(mesh):
    return jax.shard_map(
        shards,
        mesh=mesh,
        in_specs=(
            P(("tm", "head"), None),
            P("tm", "head"),
            P("tm", "head"),
            P("tm", "head"),
            P("tm", "head"),
            P("tm", "head"),
            P("head", "tm"),
        ),
        out_specs=P(("tm", "head"), None),
        check_vma=False,
    )
```

profile of v0, /device:TPU:6, one launch (start us, length us, event | category | flops | bytes accessed | tf_op | source)
XLA Modules:
  0.0 110.7 jit_solution(12447846987612990103)
XLA Ops:
  6.5 1.6 %select_select_fusion = bf16[128,640]{1,0:T(8,128)(2,1)} fusion(bf16[128,128]{1,0:T(8,128)(2,1)} %param.13, bf16[128,128]{1,0:T(8,128)(2,1)} %param.12, bf16[128,128]{1,0:T(8,128)(2,1)} %param.11, bf16[128,128]{1,0:T(8,128)(2,1)} %param.10, bf16[128,128]{1,0:T(8,128)(2,1)} %param.9, pred[640]{0:T(1024)(128)(4,1)S(1)} %get-tuple-element.47, ...), kind=kLoop, calls=%fused_computation.47 | loop fusion | flops 327680 | bytes 330240 | tf_op jit(solution)/shard_map/jit(_where)/select_n | solution.py:52
  8.1 2.5 %broadcast_in_dim.113 = bf16[16,32,2048]{2,1,0:T(8,128)(2,1)} broadcast(bf16[32,2048]{1,0:T(8,128)(2,1)} %param.7), dimensions={1,2} | broadcast | bytes 2228224 | tf_op jit(solution)/shard_map/broadcast_in_dim | solution.py:13
  10.6 7.6 %all-to-all-start = ((bf16[16,32,2048]{2,1,0:T(8,128)(2,1)}), bf16[16,32,2048]{2,1,0:T(8,128)(2,1)S(1)}, u32[]{:S(2)}, u32[]{:S(2)}) async-start(bf16[16,32,2048]{2,1,0:T(8,128)(2,1)} %broadcast_in_dim.113), calls=%async_computation | async-start | bytes 4194304 | tf_op jit(solution)/shard_map/all_to_all | solution.py:14
  23.6 22.9 %all-to-all-done = bf16[16,32,2048]{2,1,0:T(8,128)(2,1)S(1)} async-done(((bf16[16,32,2048]{2,1,0:T(8,128)(2,1)}), bf16[16,32,2048]{2,1,0:T(8,128)(2,1)S(1)}, u32[]{:S(2)}, u32[]{:S(2)}) %all-to-all-start) | async-done | bytes 2097184 | tf_op jit(solution)/shard_map/all_to_all | solution.py:14
  46.4 6.1 %all-gather.2.cloned.1.call-done = bf16[2048,640]{1,0:T(8,128)(2,1)} async-done(((bf16[128,640]{1,0:T(8,128)(2,1)}), bf16[2048,640]{1,0:T(8,128)(2,1)}) %all-gather.2.cloned.1.call-update) | async-done | bytes 2621456 | tf_op jit(solution)/shard_map/all_gather | solution.py:53
  52.6 3.8 %fusion.58 = (bf16[512,512]{1,0:T(8,128)(2,1)S(1)}, f32[512,512]{1,0:T(8,128)}) fusion(bf16[512,2048]{1,0:T(8,128)(2,1)S(1)} %bitcast.110, bf16[2048,640]{1,0:T(8,128)(2,1)} %all-gather.2.cloned.1.call-done), kind=kOutput, calls=%fused_computation.95 | convolution fusion | flops 1074003968 | bytes 5767168 | tf_op jit(solution)/shard_map/dot_general | solution.py:57
  56.9 0.9 broadcast_in_dim.122
  57.8 4.0 %all-to-all-start.1 = ((bf16[16,1,136,128]{3,2,1,0:T(8,128)(2,1)}), bf16[16,1,136,128]{3,2,1,0:T(8,128)(2,1)S(1)}, u32[]{:S(2)}, u32[]{:S(2)}) async-start(bf16[16,1,136,128]{3,2,1,0:T(8,128)(2,1)} %broadcast_in_dim.122), calls=%async_computation.1 | async-start | bytes 1114112 | tf_op jit(solution)/shard_map/all_to_all | solution.py:14
  64.4 1.1 slice.73
  65.6 1.5 %collective-permute-start.3 = (bf16[8,128,128]{2,1,0:T(8,128)(2,1)S(1)}, bf16[8,128,128]{2,1,0:T(8,128)(2,1)S(1)}, u32[]{:S(2)}, u32[]{:S(2)}) collective-permute-start(bf16[8,128,128]{2,1,0:T(8,128)(2,1)S(1)} %constant_dynamic-slice_fusion), channel_id=1, source_target_pairs={{0,2},{1,3},{2,0},{3,1},{4,6},{5,7},{6,4},{7,5},{8,10},{9,11},{10,... | collective-permute-start | bytes 786440 | tf_op jit(solution)/shard_map/ppermute | solution.py:133
  67.1 2.4 %collective-permute-start.4 = (bf16[8,128,128]{2,1,0:T(8,128)(2,1)S(1)}, bf16[8,128,128]{2,1,0:T(8,128)(2,1)S(1)}, u32[]{:S(2)}, u32[]{:S(2)}) collective-permute-start(bf16[8,128,128]{2,1,0:T(8,128)(2,1)S(1)} %constant_dynamic-slice_fusion), channel_id=1, source_target_pairs={{0,1},{1,2},{2,3},{3,0},{4,5},{5,6},{6,7},{7,4},{8,9},{9,10},{10,1... | collective-permute-start | bytes 786440 | tf_op jit(solution)/shard_map/ppermute | solution.py:133
  69.5 1.2 %fusion.15 = f32[1,512,1,128]{3,1,2,0:T(8,128)} fusion(f32[512]{0:T(512)S(1)} %get-tuple-element.22, bf16[512,512]{1,0:T(8,128)(2,1)S(1)} %get-tuple-element.43), kind=kOutput, calls=%fused_computation.16 | convolution fusion | flops 135528448 | bytes 659456 | tf_op jit(solution)/shard_map/while/body/eval_jaxpr/hts,shd->thd/dot_general | solution.py:89
  70.7 5.6 %collective-permute-done.3 = bf16[8,128,128]{2,1,0:T(8,128)(2,1)S(1)} collective-permute-done((bf16[8,128,128]{2,1,0:T(8,128)(2,1)S(1)}, bf16[8,128,128]{2,1,0:T(8,128)(2,1)S(1)}, u32[]{:S(2)}, u32[]{:S(2)}) %collective-permute-start.3) | collective-permute-done | bytes 262176 | tf_op jit(solution)/shard_map/ppermute | solution.py:133
  76.3 4.1 %collective-permute-done.4 = bf16[8,128,128]{2,1,0:T(8,128)(2,1)S(1)} collective-permute-done((bf16[8,128,128]{2,1,0:T(8,128)(2,1)S(1)}, bf16[8,128,128]{2,1,0:T(8,128)(2,1)S(1)}, u32[]{:S(2)}, u32[]{:S(2)}) %collective-permute-start.4) | collective-permute-done | bytes 262176 | tf_op jit(solution)/shard_map/ppermute | solution.py:133
  82.0 1.5 %fusion.59 = (f32[512]{0:T(512)S(1)}, f32[1,512,1,128]{3,1,2,0:T(8,128)S(1)}) fusion(f32[1,512,1,128]{3,1,2,0:T(8,128)} %fusion.15, f32[512]{0:T(512)S(1)} %exp.53, bf16[512,512]{1,0:T(8,128)(2,1)} %copy-done, f32[128,128]{1,0:T(8,128)S(1)} %multiply_reduce_fusion, f32[]{:T(128)} %bitcast.11), kind=kOutput, calls=%fused_computation.96 | convolution fusion | flops 100941312 | bytes 725504 | tf_op jit(solution)/shard_map/cthd,chde->cthe/dot_general | solution.py:106
  83.8 1.2 %fusion.32 = bf16[512,128]{1,0:T(8,128)(2,1)S(1)} fusion(f32[1,512,1,128]{3,1,2,0:T(8,128)S(1)} %get-tuple-element.46, f32[512,512]{1,0:T(8,128)} %get-tuple-element.44, f32[512]{0:T(512)S(1)} %add_sqrt_fusion, f32[512]{0:T(512)S(1)} %broadcast_multiply_fusion), kind=kLoop, calls=%fused_computation.43 | loop fusion | flops 524288 | bytes 659456 | tf_op jit(solution)/shard_map/convert_element_type | solution.py:113
  85.0 1.9 %collective-permute-start = (bf16[4,32,128]{2,1,0:T(8,128)(2,1)S(1)}, bf16[4,32,128]{2,1,0:T(8,128)(2,1)S(1)}, u32[]{:S(2)}, u32[]{:S(2)}) collective-permute-start(bf16[4,32,128]{2,1,0:T(8,128)(2,1)S(1)} %get-tuple-element.42), channel_id=1, source_target_pairs={{0,2},{1,3},{2,0},{3,1},{4,6},{5,7},{6,4},{7,5},{8,10},{9,11},{10,... | collective-permute-start | bytes 98312 | tf_op jit(solution)/shard_map/ppermute | solution.py:132
  86.9 1.8 %collective-permute-start.1 = (bf16[4,32,128]{2,1,0:T(8,128)(2,1)S(1)}, bf16[4,32,128]{2,1,0:T(8,128)(2,1)S(1)}, u32[]{:S(2)}, u32[]{:S(2)}) collective-permute-start(bf16[4,32,128]{2,1,0:T(8,128)(2,1)S(1)} %get-tuple-element.41), channel_id=1, source_target_pairs={{0,1},{1,2},{2,3},{3,0},{4,5},{5,6},{6,7},{7,4},{8,9},{9,10},{10,1... | collective-permute-start | bytes 98312 | tf_op jit(solution)/shard_map/ppermute | solution.py:132
  89.0 1.5 %collective-permute-done = bf16[4,32,128]{2,1,0:T(8,128)(2,1)S(1)} collective-permute-done((bf16[4,32,128]{2,1,0:T(8,128)(2,1)S(1)}, bf16[4,32,128]{2,1,0:T(8,128)(2,1)S(1)}, u32[]{:S(2)}, u32[]{:S(2)}) %collective-permute-start) | collective-permute-done | bytes 32800 | tf_op jit(solution)/shard_map/ppermute | solution.py:132
  90.8 3.0 %collective-permute-done.2 = bf16[4,32,128]{2,1,0:T(8,128)(2,1)S(1)} collective-permute-done((bf16[4,32,128]{2,1,0:T(8,128)(2,1)S(1)}, bf16[4,32,128]{2,1,0:T(8,128)(2,1)S(1)}, u32[]{:S(2)}, u32[]{:S(2)}) %collective-permute-start.2) | collective-permute-done | bytes 32800 | tf_op jit(solution)/shard_map/ppermute | solution.py:132
  94.4 2.2 %collective-permute-start.7 = (bf16[32,2048]{1,0:T(8,128)(2,1)S(1)}, bf16[32,2048]{1,0:T(8,128)(2,1)S(1)}, u32[]{:S(2)}, u32[]{:S(2)}) collective-permute-start(bf16[32,2048]{1,0:T(8,128)(2,1)S(1)} %get-tuple-element.25), channel_id=1, source_target_pairs={{0,8},{1,9},{2,10},{3,11},{4,12},{5,13},{6,14},{7,15},{8,0},{9,1},... | collective-permute-start | bytes 393224 | tf_op jit(solution)/shard_map/ppermute | solution.py:151
  97.2 2.6 %collective-permute-start.9 = (bf16[32,2048]{1,0:T(8,128)(2,1)S(1)}, bf16[32,2048]{1,0:T(8,128)(2,1)S(1)}, u32[]{:S(2)}, u32[]{:S(2)}) collective-permute-start(bf16[32,2048]{1,0:T(8,128)(2,1)S(1)} %get-tuple-element.26), channel_id=1, source_target_pairs={{0,12},{1,13},{2,14},{3,15},{4,0},{5,1},{6,2},{7,3},{8,4},{9,5},{1... | collective-permute-start | bytes 393224 | tf_op jit(solution)/shard_map/ppermute | solution.py:151
  99.8 1.9 %collective-permute-done.7 = bf16[32,2048]{1,0:T(8,128)(2,1)S(1)} collective-permute-done((bf16[32,2048]{1,0:T(8,128)(2,1)S(1)}, bf16[32,2048]{1,0:T(8,128)(2,1)S(1)}, u32[]{:S(2)}, u32[]{:S(2)}) %collective-permute-start.7) | collective-permute-done | bytes 131104 | tf_op jit(solution)/shard_map/ppermute | solution.py:151
  101.7 1.4 %collective-permute-done.8 = bf16[32,2048]{1,0:T(8,128)(2,1)S(1)} collective-permute-done((bf16[32,2048]{1,0:T(8,128)(2,1)S(1)}, bf16[32,2048]{1,0:T(8,128)(2,1)S(1)}, u32[]{:S(2)}, u32[]{:S(2)}) %collective-permute-start.8) | collective-permute-done | bytes 131104 | tf_op jit(solution)/shard_map/ppermute | solution.py:151
  (51 shorter events, 8.8 us)
Async XLA Ops:
  6.5 46.1 %all-gather.2.cloned.1.call-start = ((), (), s32[]{:S(2)}) async-start(), calls=%async_computation.2 | async-start | bytes 2785280 | tf_op jit(solution)/shard_map/all_gather | solution.py:53
  10.6 7.6 %copy-start.1 = (f32[512,1]{0,1:T(1,128)S(1)}, f32[512,1]{0,1:T(1,128)}, u32[]{:S(2)}) copy-start(f32[512,1]{0,1:T(1,128)} %param.8) | copy-start | bytes 6148
  10.6 35.8 %all-to-all-start = ((bf16[16,32,2048]{2,1,0:T(8,128)(2,1)}), bf16[16,32,2048]{2,1,0:T(8,128)(2,1)S(1)}, u32[]{:S(2)}, u32[]{:S(2)}) async-start(bf16[16,32,2048]{2,1,0:T(8,128)(2,1)} %broadcast_in_dim.113), calls=%async_computation | async-start | bytes 4194304 | tf_op jit(solution)/shard_map/all_to_all | solution.py:14
  56.4 14.3 %copy-start = (bf16[512,512]{1,0:T(8,128)(2,1)}, bf16[512,512]{1,0:T(8,128)(2,1)S(1)}, u32[]{:S(2)}) copy-start(bf16[512,512]{1,0:T(8,128)(2,1)S(1)} %get-tuple-element.43) | copy-start | bytes 1572868
  57.8 23.7 %all-to-all-start.1 = ((bf16[16,1,136,128]{3,2,1,0:T(8,128)(2,1)}), bf16[16,1,136,128]{3,2,1,0:T(8,128)(2,1)S(1)}, u32[]{:S(2)}, u32[]{:S(2)}) async-start(bf16[16,1,136,128]{3,2,1,0:T(8,128)(2,1)} %broadcast_in_dim.122), calls=%async_computation.1 | async-start | bytes 1114112 | tf_op jit(solution)/shard_map/all_to_all | solution.py:14
  65.6 10.8 %collective-permute-start.3 = (bf16[8,128,128]{2,1,0:T(8,128)(2,1)S(1)}, bf16[8,128,128]{2,1,0:T(8,128)(2,1)S(1)}, u32[]{:S(2)}, u32[]{:S(2)}) collective-permute-start(bf16[8,128,128]{2,1,0:T(8,128)(2,1)S(1)} %constant_dynamic-slice_fusion), channel_id=1, source_target_pairs={{0,2},{1,3},{2,0},{3,1},{4,6},{5,7},{6,4},{7,5},{8,10},{9,11},{10,... | collective-permute-start | bytes 786440 | tf_op jit(solution)/shard_map/ppermute | solution.py:133
  67.1 13.4 %collective-permute-start.4 = (bf16[8,128,128]{2,1,0:T(8,128)(2,1)S(1)}, bf16[8,128,128]{2,1,0:T(8,128)(2,1)S(1)}, u32[]{:S(2)}, u32[]{:S(2)}) collective-permute-start(bf16[8,128,128]{2,1,0:T(8,128)(2,1)S(1)} %constant_dynamic-slice_fusion), channel_id=1, source_target_pairs={{0,1},{1,2},{2,3},{3,0},{4,5},{5,6},{6,7},{7,4},{8,9},{9,10},{10,1... | collective-permute-start | bytes 786440 | tf_op jit(solution)/shard_map/ppermute | solution.py:133
  69.5 11.8 %collective-permute-start.5 = (bf16[8,128,128]{2,1,0:T(8,128)(2,1)S(1)}, bf16[8,128,128]{2,1,0:T(8,128)(2,1)S(1)}, u32[]{:S(2)}, u32[]{:S(2)}) collective-permute-start(bf16[8,128,128]{2,1,0:T(8,128)(2,1)S(1)} %constant_dynamic-slice_fusion), channel_id=1, source_target_pairs={{0,3},{1,0},{2,1},{3,2},{4,7},{5,4},{6,5},{7,6},{8,11},{9,8},{10,9... | collective-permute-start | bytes 786440 | tf_op jit(solution)/shard_map/ppermute | solution.py:133
  81.3 7.5 %collective-permute-start.6 = (bf16[3,8,128,128]{3,2,0,1:T(8,128)(2,1)S(1)}, bf16[3,8,128,128]{3,2,0,1:T(8,128)(2,1)S(1)}, u32[]{:S(2)}, u32[]{:S(2)}) collective-permute-start(bf16[3,8,128,128]{3,2,0,1:T(8,128)(2,1)S(1)} %pad_maximum_fusion), channel_id=1, source_target_pairs={{0,16},{16,0},{32,48},{48,32},{64,80},{80,64},{96,112},{112,96},{1... | collective-permute-start | bytes 2359304 | tf_op jit(solution)/shard_map/ppermute | solution.py:135
  85.0 5.5 %collective-permute-start = (bf16[4,32,128]{2,1,0:T(8,128)(2,1)S(1)}, bf16[4,32,128]{2,1,0:T(8,128)(2,1)S(1)}, u32[]{:S(2)}, u32[]{:S(2)}) collective-permute-start(bf16[4,32,128]{2,1,0:T(8,128)(2,1)S(1)} %get-tuple-element.42), channel_id=1, source_target_pairs={{0,2},{1,3},{2,0},{3,1},{4,6},{5,7},{6,4},{7,5},{8,10},{9,11},{10,... | collective-permute-start | bytes 98312 | tf_op jit(solution)/shard_map/ppermute | solution.py:132
  86.9 3.9 %collective-permute-start.1 = (bf16[4,32,128]{2,1,0:T(8,128)(2,1)S(1)}, bf16[4,32,128]{2,1,0:T(8,128)(2,1)S(1)}, u32[]{:S(2)}, u32[]{:S(2)}) collective-permute-start(bf16[4,32,128]{2,1,0:T(8,128)(2,1)S(1)} %get-tuple-element.41), channel_id=1, source_target_pairs={{0,1},{1,2},{2,3},{3,0},{4,5},{5,6},{6,7},{7,4},{8,9},{9,10},{10,1... | collective-permute-start | bytes 98312 | tf_op jit(solution)/shard_map/ppermute | solution.py:132
  88.7 5.1 %collective-permute-start.2 = (bf16[4,32,128]{2,1,0:T(8,128)(2,1)S(1)}, bf16[4,32,128]{2,1,0:T(8,128)(2,1)S(1)}, u32[]{:S(2)}, u32[]{:S(2)}) collective-permute-start(bf16[4,32,128]{2,1,0:T(8,128)(2,1)S(1)} %get-tuple-element.40), channel_id=1, source_target_pairs={{0,3},{1,0},{2,1},{3,2},{4,7},{5,4},{6,5},{7,6},{8,11},{9,8},{10,9... | collective-permute-start | bytes 98312 | tf_op jit(solution)/shard_map/ppermute | solution.py:132
  94.4 7.3 %collective-permute-start.7 = (bf16[32,2048]{1,0:T(8,128)(2,1)S(1)}, bf16[32,2048]{1,0:T(8,128)(2,1)S(1)}, u32[]{:S(2)}, u32[]{:S(2)}) collective-permute-start(bf16[32,2048]{1,0:T(8,128)(2,1)S(1)} %get-tuple-element.25), channel_id=1, source_target_pairs={{0,8},{1,9},{2,10},{3,11},{4,12},{5,13},{6,14},{7,15},{8,0},{9,1},... | collective-permute-start | bytes 393224 | tf_op jit(solution)/shard_map/ppermute | solution.py:151
  96.6 6.5 %collective-permute-start.8 = (bf16[32,2048]{1,0:T(8,128)(2,1)S(1)}, bf16[32,2048]{1,0:T(8,128)(2,1)S(1)}, u32[]{:S(2)}, u32[]{:S(2)}) collective-permute-start(bf16[32,2048]{1,0:T(8,128)(2,1)S(1)} %get-tuple-element.36), channel_id=1, source_target_pairs={{0,4},{1,5},{2,6},{3,7},{4,8},{5,9},{6,10},{7,11},{8,12},{9,13},{1... | collective-permute-start | bytes 393224 | tf_op jit(solution)/shard_map/ppermute | solution.py:151
  97.2 5.9 %collective-permute-start.9 = (bf16[32,2048]{1,0:T(8,128)(2,1)S(1)}, bf16[32,2048]{1,0:T(8,128)(2,1)S(1)}, u32[]{:S(2)}, u32[]{:S(2)}) collective-permute-start(bf16[32,2048]{1,0:T(8,128)(2,1)S(1)} %get-tuple-element.26), channel_id=1, source_target_pairs={{0,12},{1,13},{2,14},{3,15},{4,0},{5,1},{6,2},{7,3},{8,4},{9,5},{1... | collective-permute-start | bytes 393224 | tf_op jit(solution)/shard_map/ppermute | solution.py:151
Sparse Core Ops, SparseCore 0:
  9.2 43.3 all-gather.1
where the time goes:
time: 111 us
  waiting for transfers between devices  47.6 us (43%)
  starting transfers between devices  24.9 us (22%)
  between operations  17.6 us (16%)
  matrix products  7.4 us (7%)
  local copies, waits for them, and re-layouts  7.38 us (7%)
  other arithmetic  5.77 us (5%)
    all_to_all x2, waiting for transfers between devices, gather_by_exchange(): return lax.all_to_all(copies, axis, 0, 0, tiled=False)  22.9 us
    all_to_all x2, starting transfers between devices, gather_by_exchange(): return lax.all_to_all(copies, axis, 0, 0, tiled=False)  11.6 us
    ppermute x3, waiting for transfers between devices, shards(): fetched.append(lax.ppermute(own_half, 'head', across))  10.5 us
    all_gather x1, waiting for transfers between devices, shards(): stacked = lax.all_gather(packed, 'tm', axis=0, tiled=True)  6.14 us
    ppermute x3, starting transfers between devices, shards(): total = total + lax.ppermute(piece, 'head', down).astype(jnp.float32)  5.39 us
    ppermute x3, waiting for transfers between devices, shards(): pieces.append(lax.ppermute(piece, 'head', across))  4.76 us
    ppermute x3, starting transfers between devices, shards(): pieces.append(lax.ppermute(piece, 'head', across))  3.92 us
    ppermute x3, starting transfers between devices, shards(): fetched.append(lax.ppermute(own_half, 'head', across))  3.91 us
  transfers between devices with their start and end apart: 13, of which 10 were waited for; matrix products, arithmetic and copies ran while one was open for 11% of the time, Pallas kernels for 0%

commit v1 on v0

--- a/solution.py
+++ b/solution.py
@@ -6,6 +6,17 @@
 HEAD_DIM = 128
 BLOCK = 512
 PAD_ROWS = 8
+
+
+def series_all_answer(inner_x, along_dim):
+    inner_x = jnp.moveaxis(inner_x, 0, along_dim)
+    current_value = inner_x.shape
+    main = inner_x.reshape(
+        *current_value[:along_dim],
+        current_value[along_dim] * current_value[along_dim + 1],
+        *current_value[along_dim + 2 :]
+    )
+    return main
 
 
 def gather_by_exchange(part, axis):
@@ -50,7 +61,24 @@
     for start, block in reversed(list(zip(range(0, width, head_width), blocks))[:-1]):
         padded = jnp.pad(block, ((0, 0), (start, width - start - head_width)))
         packed = jnp.where(column < start + head_width, padded, packed)
-    stacked = lax.all_gather(packed, "tm", axis=0, tiled=True)
+    wide_n = lax.psum(1, axis_name="tm")
+    pieces_in = [(jj, (jj + 1) % wide_n) for jj in range(wide_n)]
+    in_order = [(k0, nth) for nth, k0 in pieces_in]
+    field_out, a_now = ([], [])
+    for b in range(wide_n - 1):
+        if b % 2 == 0:
+            small = lax.ppermute(field_out[-1] if field_out else packed, "tm", perm=pieces_in)
+            field_out.append(small)
+        else:
+            a_now.append(
+                lax.ppermute(a_now[-1] if a_now else packed, axis_name="tm", perm=in_order)
+            )
+    tmp = jnp.stack([*field_out[::-1], packed, *a_now], 0)
+    finding = lax.axis_index("tm")
+    f_next = len(field_out)
+    mixed_arr = finding - f_next
+    tmp = tmp[(jnp.arange(wide_n) - mixed_arr) % wide_n]
+    stacked = series_all_answer(tmp, 0)
     joined = stacked[:, : 4 * head_width]
     out_blocks = stacked[:, 4 * head_width :].reshape(-1, head_width, w_out.shape[1])
     frames_here = gather_by_exchange(frames, "head").reshape(-1, frames.shape[1])

time: 111 us -> 126 us (1.14)
  starting transfers between devices: 24.9 us -> 49.3 us
  local copies, waits for them, and re-layouts: 7.38 us -> 21.7 us
  between operations: 17.6 us -> 4.17 us
  waiting for transfers between devices: 47.6 us -> 37.9 us
    all_to_all x2, waiting for transfers between devices: 22.9 us -> 0.01 us  [gather_by_exchange(): return lax.all_to_all(copies, axis, 0, 0, tiled=False)]
    ppermute x0 -> x15, starting transfers between devices: none -> 21.8 us  [the longest x7 21.8 us: shards(): lax.ppermute(a_now[-1] if a_now else packed, axis_name='tm', perm=in_order)]
    ppermute x0 -> x15, waiting for transfers between devices: none -> 21 us  [the longest x8 17.3 us: shards(): lax.ppermute(field_out[-1] if field_out else packed, 'tm', perm=pieces_in)]
    unnamed x4 -> x23, local copies, waits for them, and re-layouts: 0.01 us -> 11.8 us
    all_gather x1 -> x0, waiting for transfers between devices: 6.14 us -> none  [shards(): stacked = lax.all_gather(packed, 'tm', axis=0, tiled=True)]
    gather x0 -> x1, local copies, waits for them, and re-layouts: none -> 2.76 us  [shards(): tmp = tmp[(jnp.arange(wide_n) - mixed_arr) % wide_n]]
    all_to_all x2, starting transfers between devices: 11.6 us -> 13.8 us  [gather_by_exchange(): return lax.all_to_all(copies, axis, 0, 0, tiled=False)]
  transfers between devices with their start and end apart: 13 -> 27, of which waited for: 10 -> 14; matrix products, arithmetic and copies ran while one was open for 11% -> 20% of each run, Pallas kernels for 0% -> 0%
where the time goes in v1:
time: 126 us
  starting transfers between devices  49.3 us (39%)
  waiting for transfers between devices  37.9 us (30%)
  local copies, waits for them, and re-layouts  21.7 us (17%)
  matrix products  7.66 us (6%)
  other arithmetic  5.06 us (4%)
  between operations  4.17 us (3%)
    ppermute x7, starting transfers between devices, shards(): lax.ppermute(a_now[-1] if a_now else packed, axis_name='tm', perm=in_order)  21.8 us
    ppermute x8, waiting for transfers between devices, shards(): lax.ppermute(field_out[-1] if field_out else packed, 'tm', perm=pieces_in)  17.3 us
    all_to_all x2, starting transfers between devices, gather_by_exchange(): return lax.all_to_all(copies, axis, 0, 0, tiled=False)  13.8 us
    unnamed x23, local copies, waits for them, and re-layouts  11.8 us
    ppermute x3, waiting for transfers between devices, shards(): fetched.append(lax.ppermute(own_half, 'head', across))  9.69 us
    ppermute x3, starting transfers between devices, shards(): total = total + lax.ppermute(piece, 'head', down).astype(jnp.float32)  6.29 us
    ppermute x3, waiting for transfers between devices, shards(): pieces.append(lax.ppermute(piece, 'head', across))  4.09 us
    dot_general x1, matrix products, shards(): projected = jnp.dot(frames_here, joined, preferred_element_type=jnp.float32)  3.82 us
  transfers between devices with their start and end apart: 27, of which 14 were waited for; matrix products, arithmetic and copies ran while one was open for 20% of the time, Pallas kernels for 0%

profile of v1, /device:TPU:6, one launch (start us, length us, event | category | flops | bytes accessed | tf_op | source)
XLA Modules:
  0.0 125.8 jit_solution(15182297479111206710)
XLA Ops:
  0.9 8.3 %collective-permute-done = bf16[128,640]{1,0:T(8,128)(2,1)S(1)} collective-permute-done((bf16[128,640]{1,0:T(8,128)(2,1)S(1)}, bf16[128,640]{1,0:T(8,128)(2,1)S(1)}, u32[]{:S(2)}, u32[]{:S(2)}) %collective-permute-start) | collective-permute-done | bytes 163872 | tf_op jit(solution)/shard_map/ppermute | solution.py:70
  9.2 3.0 %collective-permute-start.8 = (bf16[128,640]{1,0:T(8,128)(2,1)S(1)}, bf16[128,640]{1,0:T(8,128)(2,1)S(1)}, u32[]{:S(2)}, u32[]{:S(2)}) collective-permute-start(bf16[128,640]{1,0:T(8,128)(2,1)S(1)} %select_select_fusion), channel_id=1, source_target_pairs={{16,0},{32,16},{48,32},{64,48},{80,64},{96,80},{112,96},{128,112},... | collective-permute-start | bytes 491528 | tf_op jit(solution)/shard_map/ppermute | solution.py:74
  12.2 3.0 %collective-permute-done.1 = bf16[128,640]{1,0:T(8,128)(2,1)S(1)} collective-permute-done((bf16[128,640]{1,0:T(8,128)(2,1)S(1)}, bf16[128,640]{1,0:T(8,128)(2,1)S(1)}, u32[]{:S(2)}, u32[]{:S(2)}) %collective-permute-start.1) | collective-permute-done | bytes 163872 | tf_op jit(solution)/shard_map/ppermute | solution.py:70
  15.2 3.0 %collective-permute-start.9 = (bf16[128,640]{1,0:T(8,128)(2,1)S(1)}, bf16[128,640]{1,0:T(8,128)(2,1)S(1)}, u32[]{:S(2)}, u32[]{:S(2)}) collective-permute-start(bf16[128,640]{1,0:T(8,128)(2,1)S(1)} %collective-permute-done.8), channel_id=1, source_target_pairs={{16,0},{32,16},{48,32},{64,48},{80,64},{96,80},{112,96},{128,112},... | collective-permute-start | bytes 491528 | tf_op jit(solution)/shard_map/ppermute | solution.py:74
  18.1 3.0 %collective-permute-done.2 = bf16[128,640]{1,0:T(8,128)(2,1)S(1)} collective-permute-done((bf16[128,640]{1,0:T(8,128)(2,1)S(1)}, bf16[128,640]{1,0:T(8,128)(2,1)S(1)}, u32[]{:S(2)}, u32[]{:S(2)}) %collective-permute-start.2) | collective-permute-done | bytes 163872 | tf_op jit(solution)/shard_map/ppermute | solution.py:70
  21.1 3.0 %collective-permute-start.10 = (bf16[128,640]{1,0:T(8,128)(2,1)S(1)}, bf16[128,640]{1,0:T(8,128)(2,1)S(1)}, u32[]{:S(2)}, u32[]{:S(2)}) collective-permute-start(bf16[128,640]{1,0:T(8,128)(2,1)S(1)} %collective-permute-done.9), channel_id=1, source_target_pairs={{16,0},{32,16},{48,32},{64,48},{80,64},{96,80},{112,96},{128,112},... | collective-permute-start | bytes 491528 | tf_op jit(solution)/shard_map/ppermute | solution.py:74
  24.1 3.0 %collective-permute-done.3 = bf16[128,640]{1,0:T(8,128)(2,1)S(1)} collective-permute-done((bf16[128,640]{1,0:T(8,128)(2,1)S(1)}, bf16[128,640]{1,0:T(8,128)(2,1)S(1)}, u32[]{:S(2)}, u32[]{:S(2)}) %collective-permute-start.3) | collective-permute-done | bytes 163872 | tf_op jit(solution)/shard_map/ppermute | solution.py:70
  27.1 2.5 %broadcast_in_dim.114 = bf16[16,32,2048]{2,1,0:T(8,128)(2,1)} broadcast(bf16[32,2048]{1,0:T(8,128)(2,1)} %param.7), dimensions={1,2} | broadcast | bytes 2228224 | tf_op jit(solution)/shard_map/broadcast_in_dim | solution.py:24
  29.6 7.6 %all-to-all-start = ((bf16[16,32,2048]{2,1,0:T(8,128)(2,1)}), bf16[16,32,2048]{2,1,0:T(8,128)(2,1)}, u32[]{:S(2)}, u32[]{:S(2)}) async-start(bf16[16,32,2048]{2,1,0:T(8,128)(2,1)} %broadcast_in_dim.114), calls=%async_computation | async-start | bytes 4194304 | tf_op jit(solution)/shard_map/all_to_all | solution.py:25
  37.9 2.4 %collective-permute-start.11 = (bf16[128,640]{1,0:T(8,128)(2,1)S(1)}, bf16[128,640]{1,0:T(8,128)(2,1)S(1)}, u32[]{:S(2)}, u32[]{:S(2)}) collective-permute-start(bf16[128,640]{1,0:T(8,128)(2,1)S(1)} %collective-permute-done.10), channel_id=1, source_target_pairs={{16,0},{32,16},{48,32},{64,48},{80,64},{96,80},{112,96},{128,112},... | collective-permute-start | bytes 491528 | tf_op jit(solution)/shard_map/ppermute | solution.py:74
  43.1 3.5 %collective-permute-start.12 = (bf16[128,640]{1,0:T(8,128)(2,1)S(1)}, bf16[128,640]{1,0:T(8,128)(2,1)S(1)}, u32[]{:S(2)}, u32[]{:S(2)}) collective-permute-start(bf16[128,640]{1,0:T(8,128)(2,1)S(1)} %collective-permute-done.11), channel_id=1, source_target_pairs={{16,0},{32,16},{48,32},{64,48},{80,64},{96,80},{112,96},{128,112},... | collective-permute-start | bytes 491528 | tf_op jit(solution)/shard_map/ppermute | solution.py:74
  46.7 2.8 %collective-permute-done.12 = bf16[128,640]{1,0:T(8,128)(2,1)S(1)} collective-permute-done((bf16[128,640]{1,0:T(8,128)(2,1)S(1)}, bf16[128,640]{1,0:T(8,128)(2,1)S(1)}, u32[]{:S(2)}, u32[]{:S(2)}) %collective-permute-start.12) | collective-permute-done | bytes 163872 | tf_op jit(solution)/shard_map/ppermute | solution.py:74
  49.4 3.5 %collective-permute-start.13 = (bf16[128,640]{1,0:T(8,128)(2,1)S(1)}, bf16[128,640]{1,0:T(8,128)(2,1)S(1)}, u32[]{:S(2)}, u32[]{:S(2)}) collective-permute-start(bf16[128,640]{1,0:T(8,128)(2,1)S(1)} %collective-permute-done.12), channel_id=1, source_target_pairs={{16,0},{32,16},{48,32},{64,48},{80,64},{96,80},{112,96},{128,112},... | collective-permute-start | bytes 491528 | tf_op jit(solution)/shard_map/ppermute | solution.py:74
  55.8 3.5 %collective-permute-start.14 = (bf16[128,640]{1,0:T(8,128)(2,1)S(1)}, bf16[128,640]{1,0:T(8,128)(2,1)S(1)}, u32[]{:S(2)}, u32[]{:S(2)}) collective-permute-start(bf16[128,640]{1,0:T(8,128)(2,1)S(1)} %collective-permute-done.13), channel_id=1, source_target_pairs={{16,0},{32,16},{48,32},{64,48},{80,64},{96,80},{112,96},{128,112},... | collective-permute-start | bytes 491528 | tf_op jit(solution)/shard_map/ppermute | solution.py:74
  70.2 2.8 %gather_fusion = bf16[16,128,640]{2,1,0:T(8,128)(2,1)S(1)} fusion(bf16[16,128,640]{2,1,0:T(8,128)(2,1)} %bitcast_dynamic-update-slice_fusion, s32[1024]{0:T(1024)S(1)} %pad_clamp_fusion), kind=kCustom, calls=%fused_computation | custom fusion | bytes 5242944 | tf_op jit(solution)/shard_map/gather | solution.py:80
  73.0 3.8 %fusion.60 = (bf16[512,512]{1,0:T(8,128)(2,1)S(1)}, f32[512,512]{1,0:T(8,128)}) fusion(bf16[512,2048]{1,0:T(8,128)(2,1)} %bitcast.18, bf16[2048,640]{1,0:T(8,128)(2,1)S(1)} %bitcast.145), kind=kOutput, calls=%fused_computation.119 | convolution fusion | flops 1074003968 | bytes 5767168 | tf_op jit(solution)/shard_map/dot_general | solution.py:85
  79.0 6.2 %all-to-all-start.1 = ((bf16[16,1,136,128]{3,2,1,0:T(8,128)(2,1)}), bf16[16,1,136,128]{3,2,1,0:T(8,128)(2,1)S(1)}, u32[]{:S(2)}, u32[]{:S(2)}) async-start(bf16[16,1,136,128]{3,2,1,0:T(8,128)(2,1)} %broadcast_in_dim.123), calls=%async_computation.1 | async-start | bytes 1114112 | tf_op jit(solution)/shard_map/all_to_all | solution.py:25
  87.6 2.2 %collective-permute-start.19 = (bf16[8,128,128]{2,1,0:T(8,128)(2,1)S(1)}, bf16[8,128,128]{2,1,0:T(8,128)(2,1)S(1)}, u32[]{:S(2)}, u32[]{:S(2)}) collective-permute-start(bf16[8,128,128]{2,1,0:T(8,128)(2,1)S(1)} %constant_dynamic-slice_fusion), channel_id=1, source_target_pairs={{0,1},{1,2},{2,3},{3,0},{4,5},{5,6},{6,7},{7,4},{8,9},{9,10},{10,1... | collective-permute-start | bytes 786440 | tf_op jit(solution)/shard_map/ppermute | solution.py:161
  92.3 4.7 %collective-permute-done.18 = bf16[8,128,128]{2,1,0:T(8,128)(2,1)S(1)} collective-permute-done((bf16[8,128,128]{2,1,0:T(8,128)(2,1)S(1)}, bf16[8,128,128]{2,1,0:T(8,128)(2,1)S(1)}, u32[]{:S(2)}, u32[]{:S(2)}) %collective-permute-start.18) | collective-permute-done | bytes 262176 | tf_op jit(solution)/shard_map/ppermute | solution.py:161
  96.9 2.8 %collective-permute-done.19 = bf16[8,128,128]{2,1,0:T(8,128)(2,1)S(1)} collective-permute-done((bf16[8,128,128]{2,1,0:T(8,128)(2,1)S(1)}, bf16[8,128,128]{2,1,0:T(8,128)(2,1)S(1)}, u32[]{:S(2)}, u32[]{:S(2)}) %collective-permute-start.19) | collective-permute-done | bytes 262176 | tf_op jit(solution)/shard_map/ppermute | solution.py:161
  99.8 2.2 %collective-permute-done.20 = bf16[8,128,128]{2,1,0:T(8,128)(2,1)S(1)} collective-permute-done((bf16[8,128,128]{2,1,0:T(8,128)(2,1)S(1)}, bf16[8,128,128]{2,1,0:T(8,128)(2,1)S(1)}, u32[]{:S(2)}, u32[]{:S(2)}) %collective-permute-start.20) | collective-permute-done | bytes 262176 | tf_op jit(solution)/shard_map/ppermute | solution.py:161
  112.7 2.3 %collective-permute-done.17 = bf16[4,32,128]{2,1,0:T(8,128)(2,1)S(1)} collective-permute-done((bf16[4,32,128]{2,1,0:T(8,128)(2,1)S(1)}, bf16[4,32,128]{2,1,0:T(8,128)(2,1)S(1)}, u32[]{:S(2)}, u32[]{:S(2)}) %collective-permute-start.17) | collective-permute-done | bytes 32800 | tf_op jit(solution)/shard_map/ppermute | solution.py:160
  115.7 3.1 %collective-permute-start.22 = (bf16[32,2048]{1,0:T(8,128)(2,1)S(1)}, bf16[32,2048]{1,0:T(8,128)(2,1)S(1)}, u32[]{:S(2)}, u32[]{:S(2)}) collective-permute-start(bf16[32,2048]{1,0:T(8,128)(2,1)S(1)} %get-tuple-element.25), channel_id=1, source_target_pairs={{0,8},{1,9},{2,10},{3,11},{4,12},{5,13},{6,14},{7,15},{8,0},{9,1},... | collective-permute-start | bytes 393224 | tf_op jit(solution)/shard_map/ppermute | solution.py:179
  119.3 2.6 %collective-permute-start.24 = (bf16[32,2048]{1,0:T(8,128)(2,1)S(1)}, bf16[32,2048]{1,0:T(8,128)(2,1)S(1)}, u32[]{:S(2)}, u32[]{:S(2)}) collective-permute-start(bf16[32,2048]{1,0:T(8,128)(2,1)S(1)} %get-tuple-element.26), channel_id=1, source_target_pairs={{0,12},{1,13},{2,14},{3,15},{4,0},{5,1},{6,2},{7,3},{8,4},{9,5},{1... | collective-permute-start | bytes 393224 | tf_op jit(solution)/shard_map/ppermute | solution.py:179
  (101 shorter events, 37.0 us)
Async XLA Ops:
  0.9 8.3 %collective-permute-start = (bf16[128,640]{1,0:T(8,128)(2,1)S(1)}, bf16[128,640]{1,0:T(8,128)(2,1)S(1)}, u32[]{:S(2)}, u32[]{:S(2)}) collective-permute-start(bf16[128,640]{1,0:T(8,128)(2,1)S(1)} %select_select_fusion), channel_id=1, source_target_pairs={{0,16},{16,32},{32,48},{48,64},{64,80},{80,96},{96,112},{112,128},... | collective-permute-start | bytes 491528 | tf_op jit(solution)/shard_map/ppermute | solution.py:70
  9.2 6.0 %collective-permute-start.1 = (bf16[128,640]{1,0:T(8,128)(2,1)S(1)}, bf16[128,640]{1,0:T(8,128)(2,1)S(1)}, u32[]{:S(2)}, u32[]{:S(2)}) collective-permute-start(bf16[128,640]{1,0:T(8,128)(2,1)S(1)} %collective-permute-done), channel_id=1, source_target_pairs={{0,16},{16,32},{32,48},{48,64},{64,80},{80,96},{96,112},{112,128},... | collective-permute-start | bytes 491528 | tf_op jit(solution)/shard_map/ppermute | solution.py:70
  9.2 6.0 %collective-permute-start.8 = (bf16[128,640]{1,0:T(8,128)(2,1)S(1)}, bf16[128,640]{1,0:T(8,128)(2,1)S(1)}, u32[]{:S(2)}, u32[]{:S(2)}) collective-permute-start(bf16[128,640]{1,0:T(8,128)(2,1)S(1)} %select_select_fusion), channel_id=1, source_target_pairs={{16,0},{32,16},{48,32},{64,48},{80,64},{96,80},{112,96},{128,112},... | collective-permute-start | bytes 491528 | tf_op jit(solution)/shard_map/ppermute | solution.py:74
  15.2 6.0 %collective-permute-start.2 = (bf16[128,640]{1,0:T(8,128)(2,1)S(1)}, bf16[128,640]{1,0:T(8,128)(2,1)S(1)}, u32[]{:S(2)}, u32[]{:S(2)}) collective-permute-start(bf16[128,640]{1,0:T(8,128)(2,1)S(1)} %collective-permute-done.1), channel_id=1, source_target_pairs={{0,16},{16,32},{32,48},{48,64},{64,80},{80,96},{96,112},{112,128},... | collective-permute-start | bytes 491528 | tf_op jit(solution)/shard_map/ppermute | solution.py:70
  15.2 6.0 %collective-permute-start.9 = (bf16[128,640]{1,0:T(8,128)(2,1)S(1)}, bf16[128,640]{1,0:T(8,128)(2,1)S(1)}, u32[]{:S(2)}, u32[]{:S(2)}) collective-permute-start(bf16[128,640]{1,0:T(8,128)(2,1)S(1)} %collective-permute-done.8), channel_id=1, source_target_pairs={{16,0},{32,16},{48,32},{64,48},{80,64},{96,80},{112,96},{128,112},... | collective-permute-start | bytes 491528 | tf_op jit(solution)/shard_map/ppermute | solution.py:74
  21.1 6.0 %collective-permute-start.3 = (bf16[128,640]{1,0:T(8,128)(2,1)S(1)}, bf16[128,640]{1,0:T(8,128)(2,1)S(1)}, u32[]{:S(2)}, u32[]{:S(2)}) collective-permute-start(bf16[128,640]{1,0:T(8,128)(2,1)S(1)} %collective-permute-done.2), channel_id=1, source_target_pairs={{0,16},{16,32},{32,48},{48,64},{64,80},{80,96},{96,112},{112,128},... | collective-permute-start | bytes 491528 | tf_op jit(solution)/shard_map/ppermute | solution.py:70
  21.1 16.7 %collective-permute-start.10 = (bf16[128,640]{1,0:T(8,128)(2,1)S(1)}, bf16[128,640]{1,0:T(8,128)(2,1)S(1)}, u32[]{:S(2)}, u32[]{:S(2)}) collective-permute-start(bf16[128,640]{1,0:T(8,128)(2,1)S(1)} %collective-permute-done.9), channel_id=1, source_target_pairs={{16,0},{32,16},{48,32},{64,48},{80,64},{96,80},{112,96},{128,112},... | collective-permute-start | bytes 491528 | tf_op jit(solution)/shard_map/ppermute | solution.py:74
  27.1 13.2 %collective-permute-start.4 = (bf16[128,640]{1,0:T(8,128)(2,1)S(1)}, bf16[128,640]{1,0:T(8,128)(2,1)S(1)}, u32[]{:S(2)}, u32[]{:S(2)}) collective-permute-start(bf16[128,640]{1,0:T(8,128)(2,1)S(1)} %collective-permute-done.3), channel_id=1, source_target_pairs={{0,16},{16,32},{32,48},{48,64},{64,80},{80,96},{96,112},{112,128},... | collective-permute-start | bytes 491528 | tf_op jit(solution)/shard_map/ppermute | solution.py:70
  29.6 43.4 %all-to-all-start = ((bf16[16,32,2048]{2,1,0:T(8,128)(2,1)}), bf16[16,32,2048]{2,1,0:T(8,128)(2,1)}, u32[]{:S(2)}, u32[]{:S(2)}) async-start(bf16[16,32,2048]{2,1,0:T(8,128)(2,1)} %broadcast_in_dim.114), calls=%async_computation | async-start | bytes 4194304 | tf_op jit(solution)/shard_map/all_to_all | solution.py:25
  40.2 6.4 %collective-permute-start.5 = (bf16[128,640]{1,0:T(8,128)(2,1)S(1)}, bf16[128,640]{1,0:T(8,128)(2,1)S(1)}, u32[]{:S(2)}, u32[]{:S(2)}) collective-permute-start(bf16[128,640]{1,0:T(8,128)(2,1)S(1)} %collective-permute-done.4), channel_id=1, source_target_pairs={{0,16},{16,32},{32,48},{48,64},{64,80},{80,96},{96,112},{112,128},... | collective-permute-start | bytes 491528 | tf_op jit(solution)/shard_map/ppermute | solution.py:70
  43.1 6.4 %collective-permute-start.12 = (bf16[128,640]{1,0:T(8,128)(2,1)S(1)}, bf16[128,640]{1,0:T(8,128)(2,1)S(1)}, u32[]{:S(2)}, u32[]{:S(2)}) collective-permute-start(bf16[128,640]{1,0:T(8,128)(2,1)S(1)} %collective-permute-done.11), channel_id=1, source_target_pairs={{16,0},{32,16},{48,32},{64,48},{80,64},{96,80},{112,96},{128,112},... | collective-permute-start | bytes 491528 | tf_op jit(solution)/shard_map/ppermute | solution.py:74
  46.6 6.4 %collective-permute-start.6 = (bf16[128,640]{1,0:T(8,128)(2,1)S(1)}, bf16[128,640]{1,0:T(8,128)(2,1)S(1)}, u32[]{:S(2)}, u32[]{:S(2)}) collective-permute-start(bf16[128,640]{1,0:T(8,128)(2,1)S(1)} %collective-permute-done.5), channel_id=1, source_target_pairs={{0,16},{16,32},{32,48},{48,64},{64,80},{80,96},{96,112},{112,128},... | collective-permute-start | bytes 491528 | tf_op jit(solution)/shard_map/ppermute | solution.py:70
  49.4 6.4 %collective-permute-start.13 = (bf16[128,640]{1,0:T(8,128)(2,1)S(1)}, bf16[128,640]{1,0:T(8,128)(2,1)S(1)}, u32[]{:S(2)}, u32[]{:S(2)}) collective-permute-start(bf16[128,640]{1,0:T(8,128)(2,1)S(1)} %collective-permute-done.12), channel_id=1, source_target_pairs={{16,0},{32,16},{48,32},{64,48},{80,64},{96,80},{112,96},{128,112},... | collective-permute-start | bytes 491528 | tf_op jit(solution)/shard_map/ppermute | solution.py:74
  53.0 6.4 %collective-permute-start.7 = (bf16[128,640]{1,0:T(8,128)(2,1)S(1)}, bf16[128,640]{1,0:T(8,128)(2,1)S(1)}, u32[]{:S(2)}, u32[]{:S(2)}) collective-permute-start(bf16[128,640]{1,0:T(8,128)(2,1)S(1)} %collective-permute-done.6), channel_id=1, source_target_pairs={{0,16},{16,32},{32,48},{48,64},{64,80},{80,96},{96,112},{112,128},... | collective-permute-start | bytes 491528 | tf_op jit(solution)/shard_map/ppermute | solution.py:70
  55.8 13.7 %collective-permute-start.14 = (bf16[128,640]{1,0:T(8,128)(2,1)S(1)}, bf16[128,640]{1,0:T(8,128)(2,1)S(1)}, u32[]{:S(2)}, u32[]{:S(2)}) collective-permute-start(bf16[128,640]{1,0:T(8,128)(2,1)S(1)} %collective-permute-done.13), channel_id=1, source_target_pairs={{16,0},{32,16},{48,32},{64,48},{80,64},{96,80},{112,96},{128,112},... | collective-permute-start | bytes 491528 | tf_op jit(solution)/shard_map/ppermute | solution.py:74
  79.0 24.7 %all-to-all-start.1 = ((bf16[16,1,136,128]{3,2,1,0:T(8,128)(2,1)}), bf16[16,1,136,128]{3,2,1,0:T(8,128)(2,1)S(1)}, u32[]{:S(2)}, u32[]{:S(2)}) async-start(bf16[16,1,136,128]{3,2,1,0:T(8,128)(2,1)} %broadcast_in_dim.123), calls=%async_computation.1 | async-start | bytes 1114112 | tf_op jit(solution)/shard_map/all_to_all | solution.py:25
  86.2 10.8 %collective-permute-start.18 = (bf16[8,128,128]{2,1,0:T(8,128)(2,1)S(1)}, bf16[8,128,128]{2,1,0:T(8,128)(2,1)S(1)}, u32[]{:S(2)}, u32[]{:S(2)}) collective-permute-start(bf16[8,128,128]{2,1,0:T(8,128)(2,1)S(1)} %constant_dynamic-slice_fusion), channel_id=1, source_target_pairs={{0,2},{1,3},{2,0},{3,1},{4,6},{5,7},{6,4},{7,5},{8,10},{9,11},{10,... | collective-permute-start | bytes 786440 | tf_op jit(solution)/shard_map/ppermute | solution.py:161
  87.6 12.2 %collective-permute-start.19 = (bf16[8,128,128]{2,1,0:T(8,128)(2,1)S(1)}, bf16[8,128,128]{2,1,0:T(8,128)(2,1)S(1)}, u32[]{:S(2)}, u32[]{:S(2)}) collective-permute-start(bf16[8,128,128]{2,1,0:T(8,128)(2,1)S(1)} %constant_dynamic-slice_fusion), channel_id=1, source_target_pairs={{0,1},{1,2},{2,3},{3,0},{4,5},{5,6},{6,7},{7,4},{8,9},{9,10},{10,1... | collective-permute-start | bytes 786440 | tf_op jit(solution)/shard_map/ppermute | solution.py:161
  89.8 12.2 %collective-permute-start.20 = (bf16[8,128,128]{2,1,0:T(8,128)(2,1)S(1)}, bf16[8,128,128]{2,1,0:T(8,128)(2,1)S(1)}, u32[]{:S(2)}, u32[]{:S(2)}) collective-permute-start(bf16[8,128,128]{2,1,0:T(8,128)(2,1)S(1)} %constant_dynamic-slice_fusion), channel_id=1, source_target_pairs={{0,3},{1,0},{2,1},{3,2},{4,7},{5,4},{6,5},{7,6},{8,11},{9,8},{10,9... | collective-permute-start | bytes 786440 | tf_op jit(solution)/shard_map/ppermute | solution.py:161
  102.1 8.8 %collective-permute-start.21 = (bf16[3,8,128,128]{3,2,0,1:T(8,128)(2,1)S(1)}, bf16[3,8,128,128]{3,2,0,1:T(8,128)(2,1)S(1)}, u32[]{:S(2)}, u32[]{:S(2)}) collective-permute-start(bf16[3,8,128,128]{3,2,0,1:T(8,128)(2,1)S(1)} %pad_maximum_fusion), channel_id=1, source_target_pairs={{0,16},{16,0},{32,48},{48,32},{64,80},{80,64},{96,112},{112,96},{1... | collective-permute-start | bytes 2359304 | tf_op jit(solution)/shard_map/ppermute | solution.py:163
  107.2 5.5 %collective-permute-start.15 = (bf16[4,32,128]{2,1,0:T(8,128)(2,1)S(1)}, bf16[4,32,128]{2,1,0:T(8,128)(2,1)S(1)}, u32[]{:S(2)}, u32[]{:S(2)}) collective-permute-start(bf16[4,32,128]{2,1,0:T(8,128)(2,1)S(1)} %get-tuple-element.42), channel_id=1, source_target_pairs={{0,2},{1,3},{2,0},{3,1},{4,6},{5,7},{6,4},{7,5},{8,10},{9,11},{10,... | collective-permute-start | bytes 98312 | tf_op jit(solution)/shard_map/ppermute | solution.py:160
  115.7 7.7 %collective-permute-start.22 = (bf16[32,2048]{1,0:T(8,128)(2,1)S(1)}, bf16[32,2048]{1,0:T(8,128)(2,1)S(1)}, u32[]{:S(2)}, u32[]{:S(2)}) collective-permute-start(bf16[32,2048]{1,0:T(8,128)(2,1)S(1)} %get-tuple-element.25), channel_id=1, source_target_pairs={{0,8},{1,9},{2,10},{3,11},{4,12},{5,13},{6,14},{7,15},{8,0},{9,1},... | collective-permute-start | bytes 393224 | tf_op jit(solution)/shard_map/ppermute | solution.py:179
  118.7 6.4 %collective-permute-start.23 = (bf16[32,2048]{1,0:T(8,128)(2,1)S(1)}, bf16[32,2048]{1,0:T(8,128)(2,1)S(1)}, u32[]{:S(2)}, u32[]{:S(2)}) collective-permute-start(bf16[32,2048]{1,0:T(8,128)(2,1)S(1)} %get-tuple-element.36), channel_id=1, source_target_pairs={{0,4},{1,5},{2,6},{3,7},{4,8},{5,9},{6,10},{7,11},{8,12},{9,13},{1... | collective-permute-start | bytes 393224 | tf_op jit(solution)/shard_map/ppermute | solution.py:179
  119.3 5.8 %collective-permute-start.24 = (bf16[32,2048]{1,0:T(8,128)(2,1)S(1)}, bf16[32,2048]{1,0:T(8,128)(2,1)S(1)}, u32[]{:S(2)}, u32[]{:S(2)}) collective-permute-start(bf16[32,2048]{1,0:T(8,128)(2,1)S(1)} %get-tuple-element.26), channel_id=1, source_target_pairs={{0,12},{1,13},{2,14},{3,15},{4,0},{5,1},{6,2},{7,3},{8,4},{9,5},{1... | collective-permute-start | bytes 393224 | tf_op jit(solution)/shard_map/ppermute | solution.py:179
  (7 other events, 34.3 us)
